TPU v7x, 128 devices: a whole 4x4x4 slice. The times are simulated.
128 devices in a mesh: view: 4 (over y), block: 32 (over z, x, core).
Axes of the slice: x: 4, y: 4, z: 4, core: 2. Of those that a mesh axis runs over, the one named last changes fastest.
Arguments:
- estimate: float32 [512, 128, 256], P('block'), may hold values from 0.3 to 3
- observed: float32 [4, 512, 2, 128, 256], P('view', 'block'), may hold values from 0.2 to 5
- route_dest: int32 [4, 512], P('view', 'block'), may hold values from -1 to 31, as said below
- route_pos: int32 [4, 512], P('view', 'block'), may hold values from -1 to 15, as said below
- view_span: int32 [8, 2], P('view'), may hold values from 0 to 256, as said below
- view_count: int32 [256], P('block'), may hold values from 4 to 8, as said below
- psf_taps: float32 [8, 3, 31], P('view'), may hold values from 0 to 2, as said below
- view_weight: float32 [8], P('view'), may hold values from 1 to 4
Outputs:
- restored: float32 [512, 128, 256], P('block')
Inputs may be any that keep to these rules, and one draw needn't show every extreme that they name: `route_dest`: in each view group, every brick of one of its views that lies inside that view's sub-volume stands in exactly one slot of the group's devices, with its owner block and position (view of the group times 8 plus brick of the block); other slots hold -1. One device's slots send at most 1 bricks to one block, and some device sends 1 to some block. `route_pos`: position of the slot's brick as described for route_dest, -1 together with it. `view_span`: each sub-volume lies within the 256 bricks and holds at least 128 of them; the first view of each view group spans all of them. `view_count`: equals the number of views whose span holds the brick. `psf_taps`: each kernel is positive.
All inputs are finite; a program needn't handle non-finite values.
Results may differ from a plain program's by a relative error of at most 0.0003.
Values sent between devices are 32-bit elements; how exact they have to be, the bound alone decides.
No kernel may reach another device: no remote copies, remote signals or barrier semaphores. Data moves between devices by JAX's collectives and lax.ppermute only.
A program may use at most 128 MiB of HBM per device.

v0:
```python
import jax
import jax.numpy as jnp
from jax import lax
from jax.sharding import PartitionSpec as P

ITERS = 2


def with_halo(cells, sides, width):
    for axis, dim in sides:
        count = lax.axis_size(axis)
        ends = count - 1
        head = lax.slice_in_dim(cells, 0, width, axis=dim)
        tail = lax.slice_in_dim(cells, cells.shape[dim] - width, cells.shape[dim], axis=dim)
        cells = jnp.concatenate(
            [
                lax.ppermute(tail, axis, [(i, (i + 1) % count) for i in range(ends)]),
                cells,
                lax.ppermute(head, axis, [((i + 1) % count, i) for i in range(ends)]),
            ],
            axis=dim,
        )
    return cells


def banded_blur_matrix(filter_tap_values, row_count, col_count, offset_base, orientation):
    tap_count = filter_tap_values.shape[-1]
    grid_shape = (row_count, col_count, tap_count)
    row_index = lax.broadcasted_iota(jnp.int32, grid_shape, 0)
    col_index = lax.broadcasted_iota(jnp.int32, grid_shape, 1)
    tap_index = lax.broadcasted_iota(jnp.int32, grid_shape, 2)
    selected_entries = (orientation * (row_index - col_index) + offset_base == tap_index).astype(
        jnp.float32
    )
    return jnp.einsum(
        "ewq,gq->gew", selected_entries, filter_tap_values, precision=lax.Precision.HIGHEST
    )


def on_device(
    estimate, observed, route_dest, route_pos, view_span, view_count, psf_taps, view_weight
):
    highest = lax.Precision.HIGHEST
    blocks = lax.axis_size("block")
    slot_count = observed.shape[1]
    planes = observed.shape[2]
    ny_cells = observed.shape[3]
    nz_cells = observed.shape[4]
    per_group = view_span.shape[0]
    per_block = view_count.shape[0]
    capacity = max(1, slot_count // blocks)
    block_x = per_block * planes
    reach = psf_taps.shape[-1] // 2
    sources = observed[0]
    dest_list = route_dest[0]
    pos_list = route_pos[0]
    slot_index = jnp.arange(slot_count, dtype=jnp.int32)
    earlier = (dest_list[:, None] == dest_list[None, :]) & (
        slot_index[None, :] < slot_index[:, None]
    )
    rank_in_dest = jnp.sum(earlier.astype(jnp.int32), axis=1)
    target = jnp.where(dest_list >= 0, dest_list * capacity + rank_in_dest, blocks * capacity)
    outgoing = (
        jnp.zeros((blocks * capacity, planes, ny_cells, nz_cells), jnp.float32)
        .at[target]
        .set(sources, mode="drop")
    )
    out_pos = (
        jnp.full((blocks * capacity,), -1.0, jnp.float32)
        .at[target]
        .set(pos_list.astype(jnp.float32), mode="drop")
    )
    arrived, arrived_pos = (
        lax.all_to_all(
            outgoing.reshape(blocks, capacity, planes, ny_cells, nz_cells),
            "block",
            split_axis=0,
            concat_axis=0,
            tiled=True,
        ),
        lax.all_to_all(
            out_pos.reshape(blocks, capacity), "block", split_axis=0, concat_axis=0, tiled=True
        ),
    )
    places = arrived_pos.reshape(-1).astype(jnp.int32)
    places = jnp.where(places >= 0, places, per_group * per_block)
    placed = (
        jnp.zeros((per_group * per_block, planes, ny_cells, nz_cells), jnp.float32)
        .at[places]
        .set(arrived.reshape(-1, planes, ny_cells, nz_cells), mode="drop")
    )
    obs_views = placed.reshape(per_group, block_x, ny_cells, nz_cells)
    brick_index = lax.axis_index("block") * per_block + jnp.arange(per_block, dtype=jnp.int32)
    span_first = view_span[:, 0:1]
    span_length = view_span[:, 1:2]
    inside = (
        (brick_index[None, :] >= span_first) & (brick_index[None, :] < span_first + span_length)
    ).astype(jnp.float32)
    live_cells = jnp.repeat(inside, planes, axis=1)[:, :, None, None]
    counts = jnp.repeat(view_count.astype(jnp.float32), planes)[:, None, None]
    point_spread_kernels = psf_taps / jnp.sum(psf_taps, axis=-1, keepdims=True)
    fwd_x = banded_blur_matrix(point_spread_kernels[:, 0], block_x + 2 * reach, block_x, 0, 1)
    adj_x = banded_blur_matrix(
        point_spread_kernels[:, 0], block_x + 2 * reach, block_x, 2 * reach, -1
    )
    mat_y = banded_blur_matrix(point_spread_kernels[:, 1], ny_cells, ny_cells, reach, 1)
    mat_z = banded_blur_matrix(point_spread_kernels[:, 2], nz_cells, nz_cells, reach, 1)
    weights = view_weight[:, None, None, None]
    current = estimate
    for iteration in range(ITERS):
        padded = with_halo(current, (("block", 0),), reach)
        along_x = jnp.einsum("wyz,vwx->vxyz", padded, fwd_x, precision=highest)
        lateral_y_pass = jnp.einsum("vxyz,vyq->vxqz", along_x, mat_y, precision=highest)
        blurred = jnp.einsum("vxyz,vzq->vxyq", lateral_y_pass, mat_z, precision=highest)
        ratios = live_cells * (obs_views / blurred) + (1.0 - live_cells)
        back_z = jnp.einsum("vxyz,vqz->vxyq", ratios, mat_z, precision=highest)
        back_y = jnp.einsum("vxyz,vqy->vxqz", back_z, mat_y, precision=highest)
        rimmed = with_halo(back_y, (("block", 1),), reach)
        corrected = jnp.einsum("vwyz,vwx->vxyz", rimmed, adj_x, precision=highest)
        partial_logarithm = jnp.sum(live_cells * weights * jnp.log(corrected), axis=0)
        summed = lax.psum(partial_logarithm, "view")
        current = current * jnp.exp(summed / counts)
    return current


def solution(mesh):
    placed = (
        P("block", None, None),
        P("view", "block", None, None, None),
        P("view", "block"),
        P("view", "block"),
        P("view", None),
        P("block"),
        P("view", None, None),
        P("view"),
    )
    return jax.shard_map(
        on_device, mesh=mesh, in_specs=placed, out_specs=P("block", None, None), check_vma=False
    )
```

profile of v0, /device:TPU:1, one launch (start us, length us, event | category | flops | bytes accessed | tf_op | source)
XLA Modules:
  0.0 547.7 jit_solution(2459085685893780492)
XLA Ops:
  10.1 9.4 %all-to-all-start = ((f32[32,1,1]{2,1,0:T(1,128)}), f32[32,1,1]{2,1,0:T(1,128)S(1)}, u32[]{:S(2)}, u32[]{:S(2)}) async-start(f32[32,1,1]{2,1,0:T(1,128)} %copy.91), calls=%async_computation | async-start | bytes 32768 | tf_op jit(solution)/shard_map/all_to_all | solution.py:81
  19.5 4.2 broadcast_in_dim.37
  23.8 7.5 %scatter_fusion = f32[32,2,128,256]{3,2,1,0:T(8,128)} fusion(f32[32,2,128,256]{3,2,1,0:T(8,128)} %broadcast_in_dim.37, s32[16]{0:T(128)S(1)} %fusion.58, f32[16,2,128,256]{3,2,1,0:T(8,128)} %bitcast.92), kind=kCustom, calls=%fused_computation.1 | custom fusion | bytes 12582976 | tf_op jit(solution)/shard_map/scatter | solution.py:66
  31.2 8.0 %all-to-all-start.1 = ((f32[32,1,2,128,256]{4,3,2,1,0:T(8,128)}), f32[32,1,2,128,256]{4,3,2,1,0:T(8,128)}, u32[]{:S(2)}, u32[]{:S(2)}) async-start(f32[32,1,2,128,256]{4,3,2,1,0:T(8,128)} %bitcast.89), calls=%async_computation.1 | async-start | bytes 16777216 | tf_op jit(solution)/shard_map/all_to_all | solution.py:74
  39.4 2.3 fusion.70
  41.7 3.7 collective-permute-start
  45.4 2.4 collective-permute-start.1
  47.8 2.5 copy.103
  52.1 2.0 fusion.41
  54.9 100.3 %collective-permute-done = f32[15,128,256]{2,1,0:T(8,128)} collective-permute-done((f32[15,128,256]{2,1,0:T(8,128)}, f32[15,128,256]{2,1,0:T(8,128)}, u32[]{:S(2)}, u32[]{:S(2)}) %collective-permute-start) | collective-permute-done | bytes 1966112 | tf_op jit(solution)/shard_map/ppermute | solution.py:17
  155.2 2.7 copy.92
  157.8 1.8 collective-permute-done.1
  159.7 2.7 copy.94
  162.4 4.7 fusion.5
  167.1 17.1 %fusion.29 = f32[2,128,16,256]{3,1,2,0:T(8,128)S(1)} fusion(f32[2,128,128,1]{1,2,3,0:T(8,128)S(1)} %copy.118, f32[2,16,128,256]{3,1,2,0:T(8,128)S(1)} %fusion.5), kind=kOutput, calls=%fused_computation.37 | convolution fusion | flops 1610612736 | bytes 8519680 | tf_op jit(solution)/shard_map/vxyz,vyq->vxqz/dot_general | solution.py:113
  184.2 4.9 fusion.17
  189.1 2.5 broadcast_in_dim.33
  191.6 13.0 %scatter_fusion.1 = f32[16,2,128,256]{3,2,1,0:T(8,128)} fusion(f32[16,2,128,256]{3,2,1,0:T(8,128)} %broadcast_in_dim.33, s32[32]{0:T(128)S(1)} %fusion.57, f32[32,2,128,256]{3,2,1,0:T(8,128)} %bitcast.15), kind=kCustom, calls=%fused_computation.2 | custom fusion | bytes 25165952 | tf_op jit(solution)/shard_map/scatter | solution.py:90
  204.6 6.4 %fusion.21 = f32[2,16,128,256]{3,2,1,0:T(8,128)S(1)} fusion(f32[2,16,128,256]{3,2,1,0:T(8,128)} %fusion.17, f32[2,16]{1,0:T(2,128)S(1)} %get-tuple-element.16, f32[2,16]{1,0:T(2,128)S(1)} %broadcast_in_dim_reshape.4, f32[2,256,256,1]{2,0,1,3:T(2,128)S(1)} %fusion.41, f32[2,16,128,256]{3,2,1,0:T(8,128)} %bitcast.90), kind=kOutput, calls=%fused_computation.31 | convolution fusion | flops 3224371200 | bytes 13107456 | tf_op jit(solution)/shard_map/vxyz,vqz->vxyq/dot_general | solution.py:116
  211.0 3.8 convolution_bitcast_fusion.1
  215.7 2.0 collective-permute-start.2
  217.7 2.6 collective-permute-start.3
  220.5 39.8 %collective-permute-done.2 = f32[2,15,128,256]{3,2,1,0:T(8,128)S(1)} collective-permute-done((f32[2,15,128,256]{3,2,1,0:T(8,128)S(1)}, f32[2,15,128,256]{3,2,1,0:T(8,128)S(1)}, u32[]{:S(2)}, u32[]{:S(2)}) %collective-permute-start.2) | collective-permute-done | bytes 3932192 | tf_op jit(solution)/shard_map/ppermute | solution.py:17
  260.4 4.4 collective-permute-done.3
  264.8 2.7 pad_maximum_fusion
  267.5 13.2 %multiply_reduce_fusion.1 = f32[16,128,256]{2,0,1:T(8,128)} fusion(f32[2,46,128,256]{3,2,1,0:T(8,128)S(1)} %pad_maximum_fusion, f32[2,16]{1,0:T(2,128)S(1)} %get-tuple-element.15, f32[2,46,16,1]{1,0,2,3:T(2,128)S(1)} %convolution_bitcast_fusion.3), kind=kOutput, calls=%fused_computation.40 | convolution fusion | flops 580386816 | bytes 14161792 | tf_op jit(solution)/shard_map/vwyz,vwx->vxyz/dot_general | solution.py:119
  280.9 67.0 %all-reduce.3.cloned.1.call-done = f32[16,128,256]{2,0,1:T(8,128)} async-done(((f32[16,128,256]{2,0,1:T(8,128)}), f32[16,128,256]{2,0,1:T(8,128)}) %all-reduce.3.cloned.1.call-update) | async-done | bytes 2097168 | tf_op jit(solution)/shard_map/psum | solution.py:121
  347.9 3.6 exponential_multiply_fusion.1
  353.2 3.8 collective-permute-start.4
  358.2 2.1 collective-permute-start.5
  360.3 18.3 %collective-permute-done.4 = f32[15,128,256]{2,1,0:T(8,128)S(1)} collective-permute-done((f32[15,128,256]{2,1,0:T(8,128)S(1)}, f32[15,128,256]{2,1,0:T(8,128)S(1)}, u32[]{:S(2)}, u32[]{:S(2)}) %collective-permute-start.4) | collective-permute-done | bytes 1966112 | tf_op jit(solution)/shard_map/ppermute | solution.py:17
  378.6 1.1 copy.106
  379.7 4.4 collective-permute-done.5
  384.1 1.1 copy.107
  385.3 4.7 fusion.10
  390.0 6.3 %fusion.27 = f32[2,128,16,256]{3,1,2,0:T(8,128)S(1)} fusion(f32[2,128,128,1]{1,2,3,0:T(8,128)S(1)} %copy.118, f32[2,16,128,256]{3,1,2,0:T(8,128)S(1)} %fusion.10), kind=kOutput, calls=%fused_computation.35 | convolution fusion | flops 1610612736 | bytes 8519680 | tf_op jit(solution)/shard_map/vxyz,vyq->vxqz/dot_general | solution.py:113
  396.3 3.7 fusion.15
  400.0 4.4 fusion.25
  404.4 4.0 convolution_bitcast_fusion
  409.4 1.9 collective-permute-start.6
  411.3 2.7 collective-permute-start.7
  414.0 40.0 %collective-permute-done.6 = f32[2,15,128,256]{3,2,1,0:T(8,128)S(1)} collective-permute-done((f32[2,15,128,256]{3,2,1,0:T(8,128)S(1)}, f32[2,15,128,256]{3,2,1,0:T(8,128)S(1)}, u32[]{:S(2)}, u32[]{:S(2)}) %collective-permute-start.6) | collective-permute-done | bytes 3932192 | tf_op jit(solution)/shard_map/ppermute | solution.py:17
  454.0 4.4 collective-permute-done.7
  458.4 2.5 pad_maximum_fusion.1
  460.8 13.2 %multiply_reduce_fusion = f32[16,128,256]{2,0,1:T(8,128)} fusion(f32[2,46,128,256]{3,2,1,0:T(8,128)S(1)} %pad_maximum_fusion.1, f32[2,16]{1,0:T(2,128)S(1)} %get-tuple-element.15, f32[2,46,16,1]{1,0,2,3:T(2,128)S(1)} %convolution_bitcast_fusion.3), kind=kOutput, calls=%fused_computation.39 | convolution fusion | flops 580386816 | bytes 14161792 | tf_op jit(solution)/shard_map/vwyz,vwx->vxyz/dot_general | solution.py:119
  474.1 61.6 %all-reduce.5.cloned.1.call-done = f32[16,128,256]{2,0,1:T(8,128)} async-done(((f32[16,128,256]{2,0,1:T(8,128)}), f32[16,128,256]{2,0,1:T(8,128)}) %all-reduce.5.cloned.1.call-update) | async-done | bytes 2097168 | tf_op jit(solution)/shard_map/psum | solution.py:121
  535.7 2.1 exponential_multiply_fusion
  537.9 2.5 copy.116
  (47 shorter events, 11.2 us)
Async XLA Ops:
  10.1 21.1 %all-to-all-start = ((f32[32,1,1]{2,1,0:T(1,128)}), f32[32,1,1]{2,1,0:T(1,128)S(1)}, u32[]{:S(2)}, u32[]{:S(2)}) async-start(f32[32,1,1]{2,1,0:T(1,128)} %copy.91), calls=%async_computation | async-start | bytes 32768 | tf_op jit(solution)/shard_map/all_to_all | solution.py:81
  31.2 8.1 %copy-start.1 = (f32[16,128,256]{2,1,0:T(8,128)S(1)}, f32[16,128,256]{2,1,0:T(8,128)}, u32[]{:S(2)}) copy-start(f32[16,128,256]{2,1,0:T(8,128)} %param.8) | copy-start | bytes 6291460
  31.2 157.9 %all-to-all-start.1 = ((f32[32,1,2,128,256]{4,3,2,1,0:T(8,128)}), f32[32,1,2,128,256]{4,3,2,1,0:T(8,128)}, u32[]{:S(2)}, u32[]{:S(2)}) async-start(f32[32,1,2,128,256]{4,3,2,1,0:T(8,128)} %bitcast.89), calls=%async_computation.1 | async-start | bytes 16777216 | tf_op jit(solution)/shard_map/all_to_all | solution.py:74
  39.3 11.1 %copy-start.3 = (f32[2,3,31]{2,0,1:T(2,128)S(1)}, f32[2,3,31]{2,0,1:T(2,128)}, u32[]{:S(2)}) copy-start(f32[2,3,31]{2,0,1:T(2,128)} %param.14) | copy-start | bytes 2236
  39.3 308.6 %all-reduce.3.cloned.1.call-start = ((), (), s32[]{:S(2)}) async-start(), calls=%async_computation.2 | async-start | bytes 4194304 | tf_op jit(solution)/shard_map/psum | solution.py:121
  41.7 9.7 %copy-start.4 = (s32[2,2]{1,0:T(2,128)S(1)}, s32[2,2]{1,0:T(2,128)}, u32[]{:S(2)}) copy-start(s32[2,2]{1,0:T(2,128)} %param.12) | copy-start | bytes 52
  41.7 10.4 %copy-start.5 = (f32[2]{0:T(128)S(1)}, f32[2]{0:T(128)}, u32[]{:S(2)}) copy-start(f32[2]{0:T(128)} %param.15) | copy-start | bytes 28
  41.7 113.5 %collective-permute-start = (f32[15,128,256]{2,1,0:T(8,128)}, f32[15,128,256]{2,1,0:T(8,128)}, u32[]{:S(2)}, u32[]{:S(2)}) collective-permute-start(f32[15,128,256]{2,1,0:T(8,128)} %get-tuple-element.13), channel_id=1, source_target_pairs={{0,1},{1,2},{2,3},{3,4},{4,5},{5,6},{6,7},{7,8},{8,9},{9,10},{10,1... | collective-permute-start | bytes 5898248 | tf_op jit(solution)/shard_map/ppermute | solution.py:17
  45.4 114.3 %collective-permute-start.1 = (f32[15,128,256]{2,1,0:T(8,128)}, f32[15,128,256]{2,1,0:T(8,128)}, u32[]{:S(2)}, u32[]{:S(2)}) collective-permute-start(f32[15,128,256]{2,1,0:T(8,128)} %get-tuple-element.14), channel_id=1, source_target_pairs={{1,0},{2,1},{3,2},{4,3},{5,4},{6,5},{7,6},{8,7},{9,8},{10,9},{11,1... | collective-permute-start | bytes 5898248 | tf_op jit(solution)/shard_map/ppermute | solution.py:19
  54.2 108.2 %copy-start.2 = (f32[16,128,256]{2,0,1:T(8,128)S(1)}, f32[16,128,256]{2,0,1:T(8,128)}, u32[]{:S(2)}) copy-start(f32[16,128,256]{2,0,1:T(8,128)} %copy.103) | copy-start | bytes 6291460
  215.7 44.6 %collective-permute-start.2 = (f32[2,15,128,256]{3,2,1,0:T(8,128)S(1)}, f32[2,15,128,256]{3,2,1,0:T(8,128)S(1)}, u32[]{:S(2)}, u32[]{:S(2)}) collective-permute-start(f32[2,15,128,256]{3,2,1,0:T(8,128)S(1)} %get-tuple-element.9), channel_id=1, source_target_pairs={{0,1},{1,2},{2,3},{3,4},{4,5},{5,6},{6,7},{7,8},{8,9},{9,10},{10,1... | collective-permute-start | bytes 11796488 | tf_op jit(solution)/shard_map/ppermute | solution.py:17
  217.7 47.0 %collective-permute-start.3 = (f32[2,15,128,256]{3,2,1,0:T(8,128)S(1)}, f32[2,15,128,256]{3,2,1,0:T(8,128)S(1)}, u32[]{:S(2)}, u32[]{:S(2)}) collective-permute-start(f32[2,15,128,256]{3,2,1,0:T(8,128)S(1)} %get-tuple-element.10), channel_id=1, source_target_pairs={{1,0},{2,1},{3,2},{4,3},{5,4},{6,5},{7,6},{8,7},{9,8},{10,9},{11,1... | collective-permute-start | bytes 11796488 | tf_op jit(solution)/shard_map/ppermute | solution.py:19
  267.5 13.3 %copy-start.6 = (s32[8]{0:T(128)S(1)}, s32[8]{0:T(128)}, u32[]{:S(2)}) copy-start(s32[8]{0:T(128)} %param.13) | copy-start | bytes 100
  280.7 255.0 %all-reduce.5.cloned.1.call-start = ((), (), s32[]{:S(2)}) async-start(), calls=%async_computation.3 | async-start | bytes 4194304 | tf_op jit(solution)/shard_map/psum | solution.py:121
  353.2 25.4 %collective-permute-start.4 = (f32[15,128,256]{2,1,0:T(8,128)S(1)}, f32[15,128,256]{2,1,0:T(8,128)S(1)}, u32[]{:S(2)}, u32[]{:S(2)}) collective-permute-start(f32[15,128,256]{2,1,0:T(8,128)S(1)} %copy.104), channel_id=1, source_target_pairs={{0,1},{1,2},{2,3},{3,4},{4,5},{5,6},{6,7},{7,8},{8,9},{9,10},{10,1... | collective-permute-start | bytes 5898248 | tf_op jit(solution)/shard_map/ppermute | solution.py:17
  358.2 25.9 %collective-permute-start.5 = (f32[15,128,256]{2,1,0:T(8,128)S(1)}, f32[15,128,256]{2,1,0:T(8,128)S(1)}, u32[]{:S(2)}, u32[]{:S(2)}) collective-permute-start(f32[15,128,256]{2,1,0:T(8,128)S(1)} %copy.105), channel_id=1, source_target_pairs={{1,0},{2,1},{3,2},{4,3},{5,4},{6,5},{7,6},{8,7},{9,8},{10,9},{11,1... | collective-permute-start | bytes 5898248 | tf_op jit(solution)/shard_map/ppermute | solution.py:19
  396.3 3.7 copy-start
  409.4 44.5 %collective-permute-start.6 = (f32[2,15,128,256]{3,2,1,0:T(8,128)S(1)}, f32[2,15,128,256]{3,2,1,0:T(8,128)S(1)}, u32[]{:S(2)}, u32[]{:S(2)}) collective-permute-start(f32[2,15,128,256]{3,2,1,0:T(8,128)S(1)} %get-tuple-element.7), channel_id=1, source_target_pairs={{0,1},{1,2},{2,3},{3,4},{4,5},{5,6},{6,7},{7,8},{8,9},{9,10},{10,1... | collective-permute-start | bytes 11796488 | tf_op jit(solution)/shard_map/ppermute | solution.py:17
  411.3 47.0 %collective-permute-start.7 = (f32[2,15,128,256]{3,2,1,0:T(8,128)S(1)}, f32[2,15,128,256]{3,2,1,0:T(8,128)S(1)}, u32[]{:S(2)}, u32[]{:S(2)}) collective-permute-start(f32[2,15,128,256]{3,2,1,0:T(8,128)S(1)} %get-tuple-element.8), channel_id=1, source_target_pairs={{1,0},{2,1},{3,2},{4,3},{5,4},{6,5},{7,6},{8,7},{9,8},{10,9},{11,1... | collective-permute-start | bytes 11796488 | tf_op jit(solution)/shard_map/ppermute | solution.py:19
Sparse Core Ops, SparseCore 0:
  280.8 67.0 all-reduce.2
  474.2 61.4 all-reduce.4
where the time goes:
time: 551 us; the launch traced here: 548 us
  waiting for transfers between devices  342 us (62%)
  matrix products  89.7 us (16%)
  local copies, waits for them, and re-layouts  48.8 us (9%)
  starting transfers between devices  38.7 us (7%)
  other arithmetic  14.2 us (3%)
  between operations  14.2 us (3%)
    ppermute x4, waiting for transfers between devices, with_halo(): lax.ppermute(tail, axis, [(i, (i + 1) % count) for i in range(ends)])  198 us
    psum x2, waiting for transfers between devices, on_device(): summed = lax.psum(partial_logarithm, 'view')  129 us
    dot_general x2, matrix products, on_device(): corrected = jnp.einsum('vwyz,vwx->vxyz', rimmed, adj_x, precision=highest)  26.5 us
    dot_general x2, matrix products, on_device(): jnp.einsum('vxyz,vyq->vxqz', along_x, mat_y, precision=highest)  23.4 us
    ppermute x4, waiting for transfers between devices, with_halo(): lax.ppermute(head, axis, [((i + 1) % count, i) for i in range(ends)])  15 us
    scatter x1, local copies, waits for them, and re-layouts, on_device(): placed = jnp.zeros((per_group * per_block, planes, ny_cells, nz_cells), j...  13 us
    ppermute x4, starting transfers between devices, with_halo(): lax.ppermute(tail, axis, [(i, (i + 1) % count) for i in range(ends)])  11.4 us
  transfers between devices with their start and end apart: 12, of which 10 were waited for; matrix products, arithmetic and copies ran while one was open for 10% of the time, Pallas kernels for 0%

commit v1 on v0

--- a/solution.py
+++ b/solution.py
@@ -118,7 +118,9 @@
         rimmed = with_halo(back_y, (("block", 1),), reach)
         corrected = jnp.einsum("vwyz,vwx->vxyz", rimmed, adj_x, precision=highest)
         partial_logarithm = jnp.sum(live_cells * weights * jnp.log(corrected), axis=0)
-        summed = lax.psum(partial_logarithm, "view")
+        summed = partial_logarithm
+        for hop in (1, 2):
+            summed = summed + lax.ppermute(summed, "view", [(dev, dev ^ hop) for dev in range(4)])
         current = current * jnp.exp(summed / counts)
     return current
 

time: 551 us -> 591 us (1.073)
  the two profiles are of different devices: /device:TPU:1 before, /device:TPU:5 now
where the time goes in v1:
time: 591 us; the launch traced here: 588 us
  waiting for transfers between devices  395 us (67%)
  matrix products  76 us (13%)
  starting transfers between devices  52.5 us (9%)
  local copies, waits for them, and re-layouts  49.2 us (8%)
  other arithmetic  14.9 us (3%)
    ppermute x4, waiting for transfers between devices, with_halo(): lax.ppermute(tail, axis, [(i, (i + 1) % count) for i in range(ends)])  204 us
    ppermute x4, waiting for transfers between devices, on_device(): lax.ppermute(summed, 'view', [(dev, dev ^ hop) for dev in range(4)])  177 us
    dot_general x2, matrix products, on_device(): corrected = jnp.einsum('vwyz,vwx->vxyz', rimmed, adj_x, precision=highest)  23.9 us
    ppermute x4, starting transfers between devices, with_halo(): lax.ppermute(tail, axis, [(i, (i + 1) % count) for i in range(ends)])  17.8 us
    scatter x1, local copies, waits for them, and re-layouts, on_device(): placed = jnp.zeros((per_group * per_block, planes, ny_cells, nz_cells), j...  13.5 us
    ppermute x4, waiting for transfers between devices, with_halo(): lax.ppermute(head, axis, [((i + 1) % count, i) for i in range(ends)])  13.4 us
    dot_general x2, matrix products, on_device(): jnp.einsum('vxyz,vyq->vxqz', along_x, mat_y, precision=highest)  12.3 us
  transfers between devices with their start and end apart: 14, of which 11 were waited for; matrix products, arithmetic and copies ran while one was open for 8% of the time, Pallas kernels for 0%

profile of v1, /device:TPU:5, one launch (start us, length us, event | category | flops | bytes accessed | tf_op | source)
XLA Modules:
  0.0 587.9 jit_solution(7574191024826737545)
XLA Ops:
  3.6 8.7 %all-to-all-start = ((f32[32,1,1]{2,1,0:T(1,128)}), f32[32,1,1]{2,1,0:T(1,128)S(1)}, u32[]{:S(2)}, u32[]{:S(2)}) async-start(f32[32,1,1]{2,1,0:T(1,128)} %copy.91), calls=%async_computation | async-start | bytes 32768 | tf_op jit(solution)/shard_map/all_to_all | solution.py:81
  12.3 4.3 broadcast_in_dim.37
  16.5 7.3 %scatter_fusion = f32[32,2,128,256]{3,2,1,0:T(8,128)} fusion(f32[32,2,128,256]{3,2,1,0:T(8,128)} %broadcast_in_dim.37, s32[16]{0:T(128)S(1)} %fusion.58, f32[16,2,128,256]{3,2,1,0:T(8,128)} %bitcast.92), kind=kCustom, calls=%fused_computation.1 | custom fusion | bytes 12582976 | tf_op jit(solution)/shard_map/scatter | solution.py:66
  23.8 8.2 %all-to-all-start.1 = ((f32[32,1,2,128,256]{4,3,2,1,0:T(8,128)}), f32[32,1,2,128,256]{4,3,2,1,0:T(8,128)}, u32[]{:S(2)}, u32[]{:S(2)}) async-start(f32[32,1,2,128,256]{4,3,2,1,0:T(8,128)} %bitcast.89), calls=%async_computation.1 | async-start | bytes 16777216 | tf_op jit(solution)/shard_map/all_to_all | solution.py:74
  32.1 2.5 fusion.70
  34.6 3.2 collective-permute-start
  37.8 2.1 collective-permute-start.1
  39.9 2.5 copy.103
  44.2 2.0 fusion.41
  47.0 104.9 %collective-permute-done = f32[15,128,256]{2,1,0:T(8,128)} collective-permute-done((f32[15,128,256]{2,1,0:T(8,128)}, f32[15,128,256]{2,1,0:T(8,128)}, u32[]{:S(2)}, u32[]{:S(2)}) %collective-permute-start) | collective-permute-done | bytes 1966112 | tf_op jit(solution)/shard_map/ppermute | solution.py:17
  151.8 2.7 copy.92
  154.5 2.7 copy.94
  157.3 4.7 fusion.5
  162.0 6.3 %fusion.29 = f32[2,128,16,256]{3,1,2,0:T(8,128)S(1)} fusion(f32[2,128,128,1]{1,2,3,0:T(8,128)S(1)} %copy.118, f32[2,16,128,256]{3,1,2,0:T(8,128)S(1)} %fusion.5), kind=kOutput, calls=%fused_computation.37 | convolution fusion | flops 1610612736 | bytes 8519680 | tf_op jit(solution)/shard_map/vxyz,vyq->vxqz/dot_general | solution.py:113
  168.2 4.9 fusion.17
  173.2 2.4 broadcast_in_dim.33
  175.6 13.5 %scatter_fusion.1 = f32[16,2,128,256]{3,2,1,0:T(8,128)} fusion(f32[16,2,128,256]{3,2,1,0:T(8,128)} %broadcast_in_dim.33, s32[32]{0:T(128)S(1)} %fusion.57, f32[32,2,128,256]{3,2,1,0:T(8,128)} %bitcast.15), kind=kCustom, calls=%fused_computation.2 | custom fusion | bytes 25165952 | tf_op jit(solution)/shard_map/scatter | solution.py:90
  189.1 6.4 %fusion.21 = f32[2,16,128,256]{3,2,1,0:T(8,128)S(1)} fusion(f32[2,16,128,256]{3,2,1,0:T(8,128)} %fusion.17, f32[2,16]{1,0:T(2,128)S(1)} %get-tuple-element.16, f32[2,16]{1,0:T(2,128)S(1)} %broadcast_in_dim_reshape.4, f32[2,256,256,1]{2,0,1,3:T(2,128)S(1)} %fusion.41, f32[2,16,128,256]{3,2,1,0:T(8,128)} %bitcast.90), kind=kOutput, calls=%fused_computation.31 | convolution fusion | flops 3224371200 | bytes 13107456 | tf_op jit(solution)/shard_map/vxyz,vqz->vxyq/dot_general | solution.py:116
  195.5 3.8 convolution_bitcast_fusion.1
  200.2 4.4 collective-permute-start.2
  204.6 1.9 collective-permute-start.3
  206.8 40.5 %collective-permute-done.2 = f32[2,15,128,256]{3,2,1,0:T(8,128)S(1)} collective-permute-done((f32[2,15,128,256]{3,2,1,0:T(8,128)S(1)}, f32[2,15,128,256]{3,2,1,0:T(8,128)S(1)}, u32[]{:S(2)}, u32[]{:S(2)}) %collective-permute-start.2) | collective-permute-done | bytes 3932192 | tf_op jit(solution)/shard_map/ppermute | solution.py:17
  247.3 4.4 collective-permute-done.3
  251.7 2.5 pad_maximum_fusion
  254.1 12.0 %multiply_reduce_fusion.1 = f32[16,128,256]{2,0,1:T(8,128)S(1)} fusion(f32[2,46,128,256]{3,2,1,0:T(8,128)S(1)} %pad_maximum_fusion, f32[2,16]{1,0:T(2,128)S(1)} %get-tuple-element.15, f32[2,46,16,1]{1,0,2,3:T(2,128)S(1)} %convolution_bitcast_fusion.3), kind=kOutput, calls=%fused_computation.40 | convolution fusion | flops 580386816 | bytes 14161792 | tf_op jit(solution)/shard_map/vwyz,vwx->vxyz/dot_general | solution.py:119
  266.1 2.2 collective-permute-start.4
  268.3 42.3 %collective-permute-done.4 = f32[16,128,256]{2,0,1:T(8,128)S(1)} collective-permute-done((f32[16,128,256]{2,0,1:T(8,128)S(1)}, f32[16,128,256]{2,0,1:T(8,128)S(1)}, u32[]{:S(2)}, u32[]{:S(2)}) %collective-permute-start.4) | collective-permute-done | bytes 2097184 | tf_op jit(solution)/shard_map/ppermute | solution.py:123
  312.4 3.0 collective-permute-start.5
  315.5 43.6 %collective-permute-done.5 = f32[16,128,256]{2,0,1:T(8,128)} collective-permute-done((f32[16,128,256]{2,0,1:T(8,128)}, f32[16,128,256]{2,0,1:T(8,128)}, u32[]{:S(2)}, u32[]{:S(2)}) %collective-permute-start.5) | collective-permute-done | bytes 2097184 | tf_op jit(solution)/shard_map/ppermute | solution.py:123
  359.1 3.7 exponential_multiply_fusion.1
  364.6 8.2 %collective-permute-start.6 = (f32[15,128,256]{2,1,0:T(8,128)S(1)}, f32[15,128,256]{2,1,0:T(8,128)S(1)}, u32[]{:S(2)}, u32[]{:S(2)}) collective-permute-start(f32[15,128,256]{2,1,0:T(8,128)S(1)} %copy.104), channel_id=1, source_target_pairs={{0,1},{1,2},{2,3},{3,4},{4,5},{5,6},{6,7},{7,8},{8,9},{9,10},{10,1... | collective-permute-start | bytes 5898248 | tf_op jit(solution)/shard_map/ppermute | solution.py:17
  374.0 2.3 collective-permute-start.7
  376.3 18.1 %collective-permute-done.6 = f32[15,128,256]{2,1,0:T(8,128)S(1)} collective-permute-done((f32[15,128,256]{2,1,0:T(8,128)S(1)}, f32[15,128,256]{2,1,0:T(8,128)S(1)}, u32[]{:S(2)}, u32[]{:S(2)}) %collective-permute-start.6) | collective-permute-done | bytes 1966112 | tf_op jit(solution)/shard_map/ppermute | solution.py:17
  395.5 4.4 collective-permute-done.7
  401.1 4.7 fusion.10
  405.8 6.1 %fusion.27 = f32[2,128,16,256]{3,1,2,0:T(8,128)S(1)} fusion(f32[2,128,128,1]{1,2,3,0:T(8,128)S(1)} %copy.118, f32[2,16,128,256]{3,1,2,0:T(8,128)S(1)} %fusion.10), kind=kOutput, calls=%fused_computation.35 | convolution fusion | flops 1610612736 | bytes 8519680 | tf_op jit(solution)/shard_map/vxyz,vyq->vxqz/dot_general | solution.py:113
  411.9 3.7 fusion.15
  415.6 4.4 fusion.25
  420.0 4.0 convolution_bitcast_fusion
  426.9 2.4 collective-permute-start.9
  429.3 40.2 %collective-permute-done.8 = f32[2,15,128,256]{3,2,1,0:T(8,128)S(1)} collective-permute-done((f32[2,15,128,256]{3,2,1,0:T(8,128)S(1)}, f32[2,15,128,256]{3,2,1,0:T(8,128)S(1)}, u32[]{:S(2)}, u32[]{:S(2)}) %collective-permute-start.8) | collective-permute-done | bytes 3932192 | tf_op jit(solution)/shard_map/ppermute | solution.py:17
  469.5 4.6 collective-permute-done.9
  474.1 2.3 pad_maximum_fusion.1
  476.4 11.9 %multiply_reduce_fusion = f32[16,128,256]{2,0,1:T(8,128)S(1)} fusion(f32[2,46,128,256]{3,2,1,0:T(8,128)S(1)} %pad_maximum_fusion.1, f32[2,16]{1,0:T(2,128)S(1)} %get-tuple-element.15, f32[2,46,16,1]{1,0,2,3:T(2,128)S(1)} %convolution_bitcast_fusion.3), kind=kOutput, calls=%fused_computation.39 | convolution fusion | flops 580386816 | bytes 14161792 | tf_op jit(solution)/shard_map/vwyz,vwx->vxyz/dot_general | solution.py:119
  489.6 44.9 %collective-permute-done.10 = f32[16,128,256]{2,0,1:T(8,128)S(1)} collective-permute-done((f32[16,128,256]{2,0,1:T(8,128)S(1)}, f32[16,128,256]{2,0,1:T(8,128)S(1)}, u32[]{:S(2)}, u32[]{:S(2)}) %collective-permute-start.10) | collective-permute-done | bytes 2097184 | tf_op jit(solution)/shard_map/ppermute | solution.py:123
  535.1 2.6 collective-permute-start.11
  537.7 46.6 %collective-permute-done.11 = f32[16,128,256]{2,0,1:T(8,128)S(1)} collective-permute-done((f32[16,128,256]{2,0,1:T(8,128)S(1)}, f32[16,128,256]{2,0,1:T(8,128)S(1)}, u32[]{:S(2)}, u32[]{:S(2)}) %collective-permute-start.11) | collective-permute-done | bytes 2097184 | tf_op jit(solution)/shard_map/ppermute | solution.py:123
  585.1 2.5 copy.116
  (51 shorter events, 19.7 us)
Async XLA Ops:
  3.6 20.3 %all-to-all-start = ((f32[32,1,1]{2,1,0:T(1,128)}), f32[32,1,1]{2,1,0:T(1,128)S(1)}, u32[]{:S(2)}, u32[]{:S(2)}) async-start(f32[32,1,1]{2,1,0:T(1,128)} %copy.91), calls=%async_computation | async-start | bytes 32768 | tf_op jit(solution)/shard_map/all_to_all | solution.py:81
  23.8 8.2 %copy-start.1 = (f32[16,128,256]{2,1,0:T(8,128)S(1)}, f32[16,128,256]{2,1,0:T(8,128)}, u32[]{:S(2)}) copy-start(f32[16,128,256]{2,1,0:T(8,128)} %param.8) | copy-start | bytes 6291460
  23.8 149.3 %all-to-all-start.1 = ((f32[32,1,2,128,256]{4,3,2,1,0:T(8,128)}), f32[32,1,2,128,256]{4,3,2,1,0:T(8,128)}, u32[]{:S(2)}, u32[]{:S(2)}) async-start(f32[32,1,2,128,256]{4,3,2,1,0:T(8,128)} %bitcast.89), calls=%async_computation.1 | async-start | bytes 16777216 | tf_op jit(solution)/shard_map/all_to_all | solution.py:74
  32.1 10.3 %copy-start.3 = (f32[2,3,31]{2,0,1:T(2,128)S(1)}, f32[2,3,31]{2,0,1:T(2,128)}, u32[]{:S(2)}) copy-start(f32[2,3,31]{2,0,1:T(2,128)} %param.14) | copy-start | bytes 2236
  34.6 8.9 %copy-start.4 = (s32[2,2]{1,0:T(2,128)S(1)}, s32[2,2]{1,0:T(2,128)}, u32[]{:S(2)}) copy-start(s32[2,2]{1,0:T(2,128)} %param.12) | copy-start | bytes 52
  34.6 9.6 %copy-start.5 = (f32[2]{0:T(128)S(1)}, f32[2]{0:T(128)}, u32[]{:S(2)}) copy-start(f32[2]{0:T(128)} %param.15) | copy-start | bytes 28
  34.6 117.3 %collective-permute-start = (f32[15,128,256]{2,1,0:T(8,128)}, f32[15,128,256]{2,1,0:T(8,128)}, u32[]{:S(2)}, u32[]{:S(2)}) collective-permute-start(f32[15,128,256]{2,1,0:T(8,128)} %get-tuple-element.13), channel_id=1, source_target_pairs={{0,1},{1,2},{2,3},{3,4},{4,5},{5,6},{6,7},{7,8},{8,9},{9,10},{10,1... | collective-permute-start | bytes 5898248 | tf_op jit(solution)/shard_map/ppermute | solution.py:17
  37.8 116.8 %collective-permute-start.1 = (f32[15,128,256]{2,1,0:T(8,128)}, f32[15,128,256]{2,1,0:T(8,128)}, u32[]{:S(2)}, u32[]{:S(2)}) collective-permute-start(f32[15,128,256]{2,1,0:T(8,128)} %get-tuple-element.14), channel_id=1, source_target_pairs={{1,0},{2,1},{3,2},{4,3},{5,4},{6,5},{7,6},{8,7},{9,8},{10,9},{11,1... | collective-permute-start | bytes 5898248 | tf_op jit(solution)/shard_map/ppermute | solution.py:19
  46.3 111.0 %copy-start.2 = (f32[16,128,256]{2,0,1:T(8,128)S(1)}, f32[16,128,256]{2,0,1:T(8,128)}, u32[]{:S(2)}) copy-start(f32[16,128,256]{2,0,1:T(8,128)} %copy.103) | copy-start | bytes 6291460
  200.2 47.0 %collective-permute-start.2 = (f32[2,15,128,256]{3,2,1,0:T(8,128)S(1)}, f32[2,15,128,256]{3,2,1,0:T(8,128)S(1)}, u32[]{:S(2)}, u32[]{:S(2)}) collective-permute-start(f32[2,15,128,256]{3,2,1,0:T(8,128)S(1)} %get-tuple-element.9), channel_id=1, source_target_pairs={{0,1},{1,2},{2,3},{3,4},{4,5},{5,6},{6,7},{7,8},{8,9},{9,10},{10,1... | collective-permute-start | bytes 11796488 | tf_op jit(solution)/shard_map/ppermute | solution.py:17
  204.6 47.0 %collective-permute-start.3 = (f32[2,15,128,256]{3,2,1,0:T(8,128)S(1)}, f32[2,15,128,256]{3,2,1,0:T(8,128)S(1)}, u32[]{:S(2)}, u32[]{:S(2)}) collective-permute-start(f32[2,15,128,256]{3,2,1,0:T(8,128)S(1)} %get-tuple-element.10), channel_id=1, source_target_pairs={{1,0},{2,1},{3,2},{4,3},{5,4},{6,5},{7,6},{8,7},{9,8},{10,9},{11,1... | collective-permute-start | bytes 11796488 | tf_op jit(solution)/shard_map/ppermute | solution.py:19
  266.1 49.3 %copy-start.6 = (s32[8]{0:T(128)S(1)}, s32[8]{0:T(128)}, u32[]{:S(2)}) copy-start(s32[8]{0:T(128)} %param.13) | copy-start | bytes 100
  266.1 44.5 %collective-permute-start.4 = (f32[16,128,256]{2,0,1:T(8,128)S(1)}, f32[16,128,256]{2,0,1:T(8,128)S(1)}, u32[]{:S(2)}, u32[]{:S(2)}) collective-permute-start(f32[16,128,256]{2,0,1:T(8,128)S(1)} %multiply_reduce_fusion.1), channel_id=1, source_target_pairs={{0,32},{32,0},{64,96},{96,64},{1,33},{33,1},{65,97},{97,65},{2,34}... | collective-permute-start | bytes 6291464 | tf_op jit(solution)/shard_map/ppermute | solution.py:123
  312.4 46.7 %collective-permute-start.5 = (f32[16,128,256]{2,0,1:T(8,128)}, f32[16,128,256]{2,0,1:T(8,128)}, u32[]{:S(2)}, u32[]{:S(2)}) collective-permute-start(f32[16,128,256]{2,0,1:T(8,128)} %add.103), channel_id=1, source_target_pairs={{0,64},{32,96},{64,0},{96,32},{1,65},{33,97},{65,1},{97,33},{2,66}... | collective-permute-start | bytes 6291464 | tf_op jit(solution)/shard_map/ppermute | solution.py:123
  364.6 29.8 %collective-permute-start.6 = (f32[15,128,256]{2,1,0:T(8,128)S(1)}, f32[15,128,256]{2,1,0:T(8,128)S(1)}, u32[]{:S(2)}, u32[]{:S(2)}) collective-permute-start(f32[15,128,256]{2,1,0:T(8,128)S(1)} %copy.104), channel_id=1, source_target_pairs={{0,1},{1,2},{2,3},{3,4},{4,5},{5,6},{6,7},{7,8},{8,9},{9,10},{10,1... | collective-permute-start | bytes 5898248 | tf_op jit(solution)/shard_map/ppermute | solution.py:17
  374.0 25.9 %collective-permute-start.7 = (f32[15,128,256]{2,1,0:T(8,128)S(1)}, f32[15,128,256]{2,1,0:T(8,128)S(1)}, u32[]{:S(2)}, u32[]{:S(2)}) collective-permute-start(f32[15,128,256]{2,1,0:T(8,128)S(1)} %copy.105), channel_id=1, source_target_pairs={{1,0},{2,1},{3,2},{4,3},{5,4},{6,5},{7,6},{8,7},{9,8},{10,9},{11,1... | collective-permute-start | bytes 5898248 | tf_op jit(solution)/shard_map/ppermute | solution.py:19
  411.9 3.7 copy-start
  424.9 44.5 %collective-permute-start.8 = (f32[2,15,128,256]{3,2,1,0:T(8,128)S(1)}, f32[2,15,128,256]{3,2,1,0:T(8,128)S(1)}, u32[]{:S(2)}, u32[]{:S(2)}) collective-permute-start(f32[2,15,128,256]{3,2,1,0:T(8,128)S(1)} %get-tuple-element.7), channel_id=1, source_target_pairs={{0,1},{1,2},{2,3},{3,4},{4,5},{5,6},{6,7},{7,8},{8,9},{9,10},{10,1... | collective-permute-start | bytes 11796488 | tf_op jit(solution)/shard_map/ppermute | solution.py:17
  426.9 47.2 %collective-permute-start.9 = (f32[2,15,128,256]{3,2,1,0:T(8,128)S(1)}, f32[2,15,128,256]{3,2,1,0:T(8,128)S(1)}, u32[]{:S(2)}, u32[]{:S(2)}) collective-permute-start(f32[2,15,128,256]{3,2,1,0:T(8,128)S(1)} %get-tuple-element.8), channel_id=1, source_target_pairs={{1,0},{2,1},{3,2},{4,3},{5,4},{6,5},{7,6},{8,7},{9,8},{10,9},{11,1... | collective-permute-start | bytes 11796488 | tf_op jit(solution)/shard_map/ppermute | solution.py:19
  488.3 46.3 %collective-permute-start.10 = (f32[16,128,256]{2,0,1:T(8,128)S(1)}, f32[16,128,256]{2,0,1:T(8,128)S(1)}, u32[]{:S(2)}, u32[]{:S(2)}) collective-permute-start(f32[16,128,256]{2,0,1:T(8,128)S(1)} %multiply_reduce_fusion), channel_id=1, source_target_pairs={{0,32},{32,0},{64,96},{96,64},{1,33},{33,1},{65,97},{97,65},{2,34}... | collective-permute-start | bytes 6291464 | tf_op jit(solution)/shard_map/ppermute | solution.py:123
  535.1 49.2 %collective-permute-start.11 = (f32[16,128,256]{2,0,1:T(8,128)S(1)}, f32[16,128,256]{2,0,1:T(8,128)S(1)}, u32[]{:S(2)}, u32[]{:S(2)}) collective-permute-start(f32[16,128,256]{2,0,1:T(8,128)S(1)} %add.106), channel_id=1, source_target_pairs={{0,64},{32,96},{64,0},{96,32},{1,65},{33,97},{65,1},{97,33},{2,66}... | collective-permute-start | bytes 6291464 | tf_op jit(solution)/shard_map/ppermute | solution.py:123
